TPU v7x, 512 devices: a whole 4x4x16 slice. The times are simulated.
512 devices in a mesh: space: 64 (over z_lo, x, core), ky: 8 (over z_hi, y).
Axes of the slice: x: 4, y: 4, z: 16 (z_hi: 2, z_lo: 8; z = z_hi * 8 + z_lo), core: 2. Of those that a mesh axis runs over, the one named last changes fastest.
Arguments:
- distribution: float32 [64, 128, 256, 128], P('space', 'ky'), may hold values from 0 to 2
- region: int32 [64, 256], P('space'), may hold values from 0 to 5, as said below
- region_doping: float32 [6], replicated, may hold values from -1 to 2
- region_relax: float32 [6], replicated, may hold values from 0.2 to 1
- equilibrium: float32 [128, 128], P('ky'), may hold values from 0.3 to 3
- kx_speed: float32 [128], replicated, may hold values from 0.1 to 1
- upwind_sign: int32 [128], replicated, may hold values from -1 to 1, as said below
Outputs:
- advanced: float32 [64, 128, 256, 128], P('space', 'ky')
Inputs may be any that keep to these rules, and one draw needn't show every extreme that they name: region[x, y] = 2 band(y) + m[x, y], with m[x, y] 0 or 1 and band(y) = 0, 1, 2 on three runs of columns, each run at least 32 columns long. `upwind_sign`: exactly 64 entries are 1 and the others -1.
All inputs are finite; a program needn't handle non-finite values.
Results may differ from a plain program's by a relative error of at most 0.0003.
Values sent between devices are 32-bit elements; how exact they have to be, the bound alone decides.
No kernel may reach another device: no remote copies, remote signals or barrier semaphores. Data moves between devices by JAX's collectives and lax.ppermute only.
A program may use at most 64 MiB of HBM per device.

v0:
```python
import math
import jax
import jax.numpy as jnp
from jax import lax
from jax.sharding import PartitionSpec as P

COUPLING = 0.04
POISSON = 0.1
STEP = 0.4
DRIFT_Y = 0.8


def with_halo(block, sides, width):
    for axis, dim in sides:
        count = lax.axis_size(axis)
        forward = [(i, i + 1) for i in range(count - 1)]
        backward = [(target, source) for source, target in forward]
        low = lax.ppermute(
            lax.slice_in_dim(block, block.shape[dim] - width, None, axis=dim), axis, forward
        )
        high = lax.ppermute(lax.slice_in_dim(block, 0, width, axis=dim), axis, backward)
        block = jnp.concatenate([low, block, high], axis=dim)
    return block


def sine_table(length):
    positions = jnp.arange(1, length + 1, dtype=jnp.int32)
    phase_index = positions[:, None] * positions[None, :] % (2 * length + 2)
    return jnp.sqrt(2.0 / (length + 1.0)) * jnp.sin(
        math.pi * phase_index.astype(jnp.float32) / (length + 1.0)
    )


def eigen_values(length):
    positions = jnp.arange(1, length + 1, dtype=jnp.int32).astype(jnp.float32)
    return 4.0 * jnp.sin(0.5 * math.pi * positions / (length + 1.0)) ** 2


def wigner_tables(modes):
    half_count = modes // 2
    shifts = jnp.arange(1, half_count + 1, dtype=jnp.int32)
    wave_index = jnp.arange(modes, dtype=jnp.int32)
    phase_index = shifts[:, None] * wave_index[None, :] % modes
    angles = 2.0 * math.pi / modes * phase_index.astype(jnp.float32)
    forward = jnp.concatenate([jnp.cos(angles), jnp.sin(angles)], axis=0)
    backward = jnp.concatenate([jnp.sin(angles).T, -jnp.cos(angles).T], axis=1)
    return (forward, backward)


def own_differences(potential, modes, first_col, local_cols):
    half_count = modes // 2
    padded = jnp.pad(potential, ((0, 0), (half_count, half_count)))
    window = lax.dynamic_slice_in_dim(padded, first_col, local_cols + 2 * half_count, 1)
    pieces = []
    for offset in range(1, half_count + 1):
        ahead_vals = window[:, half_count + offset : half_count + offset + local_cols]
        behind = window[:, half_count - offset : half_count - offset + local_cols]
        pieces.append(ahead_vals - behind)
    return COUPLING * jnp.stack(pieces, axis=1)


def lookup(region, values_table):
    classes = jnp.arange(values_table.shape[0], dtype=jnp.int32)
    return jnp.sum(jnp.where(region[..., None] == classes, values_table, 0.0), axis=-1)


def shards(distribution, region, region_doping, region_relax, equilibrium, kx_speed, upwind_sign):
    precise = lax.Precision.HIGHEST
    triple = lax.Precision.HIGH
    row_count, ky_local, col_count, kx_count = distribution.shape
    ky_count = ky_local * lax.axis_size("ky")
    grid_rows = row_count * lax.axis_size("space")
    row_start = lax.axis_index("space") * row_count
    partial_value = jnp.sum(distribution, axis=(1, 3)) / (ky_count * kx_count)
    density = lax.psum(partial_value, "ky")
    doping = lookup(region, region_doping)
    relax_rate = lookup(region, region_relax)
    charge = density - doping
    sine_rows = sine_table(grid_rows)
    sine_cols = sine_table(col_count)
    eigen_cols = eigen_values(col_count)
    every_row = lax.all_gather(charge, "space", axis=0, tiled=True)
    along_x = jnp.dot(sine_rows, every_row, precision=precise)
    spectral = jnp.dot(along_x, sine_cols, precision=precise)
    spectral = spectral / (eigen_values(grid_rows)[:, None] + eigen_cols[None, :])
    back_cols = jnp.dot(spectral, sine_cols, precision=precise)
    own_rows = lax.dynamic_slice_in_dim(sine_rows, row_start, row_count, 0)
    potential = POISSON * jnp.dot(own_rows, back_cols, precision=precise)
    spread = lax.all_to_all(distribution, "ky", split_axis=2, concat_axis=1, tiled=True)
    local_cols = spread.shape[2]
    forward, backward = wigner_tables(ky_count)
    weights = own_differences(potential, ky_count, lax.axis_index("ky") * local_cols, local_cols)
    flattened = spread.reshape(row_count, ky_count, local_cols * kx_count)
    coeffs = jnp.einsum("ab,rbm->ram", forward, flattened, precision=triple)
    coeffs = coeffs.reshape(row_count, ky_count, local_cols, kx_count)
    scaled = coeffs * jnp.concatenate([weights, weights], axis=1)[..., None]
    mixed = jnp.einsum(
        "ab,rbm->ram",
        backward,
        scaled.reshape(row_count, ky_count, local_cols * kx_count),
        precision=triple,
    )
    mixed = mixed.reshape(row_count, ky_count, local_cols, kx_count)
    wigner = lax.all_to_all(mixed, "ky", split_axis=1, concat_axis=2, tiled=True)
    positive_kx = upwind_sign > 0
    padded = with_halo(distribution, (("space", 0),), 1)
    from_left = padded[:-2]
    from_right = padded[2:]
    upstream_x = jnp.where(positive_kx[None, None, None, :], from_left, from_right)
    drift_x = -kx_speed[None, None, None, :] * (distribution - upstream_x)
    ky_global = lax.axis_index("ky") * ky_local + jnp.arange(ky_local, dtype=jnp.int32)
    upward = ky_global >= ky_count // 2
    vertical = DRIFT_Y * (ky_global.astype(jnp.float32) + 0.5 - 0.5 * ky_count) / (0.5 * ky_count)
    zero_col = jnp.zeros_like(distribution[:, :, :1])
    from_low = jnp.concatenate([zero_col, distribution[:, :, :-1]], axis=2)
    from_high = jnp.concatenate([distribution[:, :, 1:], zero_col], axis=2)
    upstream_y = jnp.where(upward[None, :, None, None], from_low, from_high)
    drift_y = -jnp.abs(vertical)[None, :, None, None] * (distribution - upstream_y)
    relaxation = relax_rate[:, None, :, None] * (
        density[:, None, :, None] * equilibrium[None, :, None, :] - distribution
    )
    return distribution + STEP * (drift_x + drift_y + wigner + relaxation)


def solution(mesh):
    return jax.shard_map(
        shards,
        mesh=mesh,
        in_specs=(
            P("space", "ky", None, None),
            P("space", None),
            P(),
            P(),
            P("ky", None),
            P(),
            P(),
        ),
        out_specs=P("space", "ky", None, None),
        check_vma=False,
    )
```

profile of v0, /device:TPU:32, one launch (start us, length us, event | category | flops | bytes accessed | tf_op | source)
XLA Modules:
  0.0 378.6 jit_solution(6376607305004779924)
XLA Ops:
  0.0 4.1 %copy.28 = f32[1,16,256,128]{3,1,0,2:T(8,128)} copy(f32[1,16,256,128]{3,2,1,0:T(8,128)} %param.7) | data formatting | bytes 4194304 | tf_op args[0]
  4.1 17.0 %all-to-all-start = ((f32[1,16,256,128]{3,1,0,2:T(8,128)}), f32[1,16,256,128]{3,1,0,2:T(8,128)}, u32[]{:S(2)}, u32[]{:S(2)}) async-start(f32[1,16,256,128]{3,1,0,2:T(8,128)} %copy.28), calls=%async_computation | async-start | bytes 4194304 | tf_op jit(solution)/shard_map/all_to_all | solution.py:89
  21.3 117.8 %psum.7 = f32[1,256]{1,0:T(1,128)S(1)} all-reduce(f32[1,256]{1,0:T(1,128)S(1)} %bitcast.205), channel_id=1, replica_groups=mesh['space'=64,'ky'=8] {'ky'}, use_global_device_ids=true, to_apply=%region_1.0 | all-reduce | flops 256 | bytes 2048 | tf_op jit(solution)/shard_map/psum | solution.py:75
  139.3 105.4 %all-gather = f32[64,1,256]{2,1,0:T(1,128)S(1)} all-gather(f32[1,1,256]{2,1,0:T(1,128)S(1)} %subtract_bitcast_fusion), channel_id=1, replica_groups=mesh['space'=64,'ky'=8] {'space'}, dimensions={0}, use_global_device_ids=true | all-gather | bytes 66560 | tf_op jit(solution)/shard_map/all_gather | solution.py:82
  245.0 0.4 fusion.39
  245.3 1.3 convolution_divide_fusion
  246.7 1.3 fusion.14
  255.7 0.3 stack.259
  256.3 1.9 mul.263
  258.2 2.7 mul.264
  261.1 0.3 fusion.54
  261.5 2.4 copy.29
  263.8 2.2 fusion.1
  266.0 3.2 fusion.35
  269.2 3.1 copy.95
  272.3 7.1 %all-to-all-start.1 = ((f32[1,128,32,128]{3,2,0,1:T(8,128)}), f32[1,128,32,128]{3,2,0,1:T(8,128)}, u32[]{:S(2)}, u32[]{:S(2)}) async-start(f32[1,128,32,128]{3,2,0,1:T(8,128)} %copy.95), calls=%async_computation.1 | async-start | bytes 4194304 | tf_op jit(solution)/shard_map/all_to_all | solution.py:104
  279.4 2.4 collective-permute-start.1
  281.8 1.9 collective-permute-start
  283.9 2.5 fusion.209
  286.3 46.5 %all-to-all-done.1 = f32[1,128,32,128]{3,2,0,1:T(8,128)} async-done(((f32[1,128,32,128]{3,2,0,1:T(8,128)}), f32[1,128,32,128]{3,2,0,1:T(8,128)}, u32[]{:S(2)}, u32[]{:S(2)}) %all-to-all-start.1) | async-done | bytes 2097184 | tf_op jit(solution)/shard_map/all_to_all | solution.py:104
  332.9 2.0 copy.96
  334.8 29.5 %collective-permute-done.1 = f32[1,16,256,128]{3,2,1,0:T(8,128)} collective-permute-done((f32[1,16,256,128]{3,2,1,0:T(8,128)S(1)}, f32[1,16,256,128]{3,2,1,0:T(8,128)}, u32[]{:S(2)}, u32[]{:S(2)}) %collective-permute-start.1) | collective-permute-done | bytes 2097184 | tf_op jit(solution)/shard_map/ppermute | solution.py:21
  364.3 8.7 %collective-permute-done = f32[1,16,256,128]{3,2,1,0:T(8,128)} collective-permute-done((f32[1,16,256,128]{3,2,1,0:T(8,128)S(1)}, f32[1,16,256,128]{3,2,1,0:T(8,128)}, u32[]{:S(2)}, u32[]{:S(2)}) %collective-permute-start) | collective-permute-done | bytes 2097184 | tf_op jit(solution)/shard_map/ppermute | solution.py:18
  373.1 5.5 %fusion.6 = f32[1,16,256,128]{3,2,1,0:T(8,128)} fusion(f32[1,16,256,128]{3,2,1,0:T(8,128)S(1)} %copy-done, f32[1,16,8,32,128]{4,3,2,1,0:T(8,128)S(1)} %copy.96, f32[1,16,255,128]{3,2,1,0:T(8,128)S(1)} %copy-done.3, f32[1,16,255,128]{3,2,1,0:T(8,128)S(1)} %copy-done.2, f32[1,16,256,128]{3,2,1,0:T(8,128)} %collective-permute-done, ...), kind=kLoop, calls=%fused_computation.8 | loop fusion | flops 7340032 | bytes 14674640 | tf_op jit(solution)/shard_map/add | solution.py:122
  (120 shorter events, 8.7 us)
Async XLA Ops:
  4.1 17.0 %copy-start = (f32[1,16,256,128]{3,2,1,0:T(8,128)S(1)}, f32[1,16,256,128]{3,2,1,0:T(8,128)}, u32[]{:S(2)}) copy-start(f32[1,16,256,128]{3,2,1,0:T(8,128)} %param.7) | copy-start | bytes 6291460
  4.1 257.3 %all-to-all-start = ((f32[1,16,256,128]{3,1,0,2:T(8,128)}), f32[1,16,256,128]{3,1,0,2:T(8,128)}, u32[]{:S(2)}, u32[]{:S(2)}) async-start(f32[1,16,256,128]{3,1,0,2:T(8,128)} %copy.28), calls=%async_computation | async-start | bytes 4194304 | tf_op jit(solution)/shard_map/all_to_all | solution.py:89
  21.1 118.1 %copy-start.5 = (s32[1,256]{1,0:T(1,128)S(1)}, s32[1,256]{1,0:T(1,128)}, u32[]{:S(2)}) copy-start(s32[1,256]{1,0:T(1,128)} %param.8) | copy-start | bytes 3076
  21.1 118.1 %copy-start.6 = (f32[6]{0:T(128)S(1)}, f32[6]{0:T(128)}, u32[]{:S(2)}) copy-start(f32[6]{0:T(128)} %param.10) | copy-start | bytes 76
  21.1 118.0 %copy-start.7 = (f32[6]{0:T(128)S(1)}, f32[6]{0:T(128)}, u32[]{:S(2)}) copy-start(f32[6]{0:T(128)} %param.9) | copy-start | bytes 76
  261.4 2.4 copy-start.1
  272.3 11.4 %copy-start.8 = (f32[128]{0:T(128)S(1)}, f32[128]{0:T(128)}, u32[]{:S(2)}) copy-start(f32[128]{0:T(128)} %param.12) | copy-start | bytes 1540
  272.3 11.5 %copy-start.9 = (s32[128]{0:T(128)S(1)}, s32[128]{0:T(128)}, u32[]{:S(2)}) copy-start(s32[128]{0:T(128)} %param.13) | copy-start | bytes 1540
  272.3 60.5 %all-to-all-start.1 = ((f32[1,128,32,128]{3,2,0,1:T(8,128)}), f32[1,128,32,128]{3,2,0,1:T(8,128)}, u32[]{:S(2)}, u32[]{:S(2)}) async-start(f32[1,128,32,128]{3,2,0,1:T(8,128)} %copy.95), calls=%async_computation.1 | async-start | bytes 4194304 | tf_op jit(solution)/shard_map/all_to_all | solution.py:104
  279.4 84.9 %collective-permute-start.1 = (f32[1,16,256,128]{3,2,1,0:T(8,128)S(1)}, f32[1,16,256,128]{3,2,1,0:T(8,128)}, u32[]{:S(2)}, u32[]{:S(2)}) collective-permute-start(f32[1,16,256,128]{3,2,1,0:T(8,128)S(1)} %copy-done), channel_id=1, source_target_pairs={{8,0},{16,8},{24,16},{32,24},{40,32},{48,40},{56,48},{64,56},{72,6... | collective-permute-start | bytes 6291464 | tf_op jit(solution)/shard_map/ppermute | solution.py:21
  281.8 91.2 %collective-permute-start = (f32[1,16,256,128]{3,2,1,0:T(8,128)S(1)}, f32[1,16,256,128]{3,2,1,0:T(8,128)}, u32[]{:S(2)}, u32[]{:S(2)}) collective-permute-start(f32[1,16,256,128]{3,2,1,0:T(8,128)S(1)} %copy-done), channel_id=1, source_target_pairs={{0,8},{8,16},{16,24},{24,32},{32,40},{40,48},{48,56},{56,64},{64,7... | collective-permute-start | bytes 6291464 | tf_op jit(solution)/shard_map/ppermute | solution.py:18
  283.8 89.2 %copy-start.4 = (f32[16,128]{1,0:T(8,128)S(1)}, f32[16,128]{1,0:T(8,128)}, u32[]{:S(2)}) copy-start(f32[16,128]{1,0:T(8,128)} %param.11) | copy-start | bytes 24580
  332.9 40.2 %copy-start.2 = (f32[1,16,255,128]{3,2,1,0:T(8,128)S(1)}, f32[1,16,255,128]{3,2,1,0:T(8,128)}, u32[]{:S(2)}) copy-start(f32[1,16,255,128]{3,2,1,0:T(8,128)} %get-tuple-element.7) | copy-start | bytes 6266884
  332.9 40.2 %copy-start.3 = (f32[1,16,255,128]{3,2,1,0:T(8,128)S(1)}, f32[1,16,255,128]{3,2,1,0:T(8,128)}, u32[]{:S(2)}) copy-start(f32[1,16,255,128]{3,2,1,0:T(8,128)} %get-tuple-element.8) | copy-start | bytes 6266884
where the time goes:
time: 379 us
  blocking collectives  223 us (59%)
  waiting for transfers between devices  84.8 us (22%)
  starting transfers between devices  28.4 us (7%)
  local copies, waits for them, and re-layouts  24.8 us (7%)
  other arithmetic  8.64 us (2%)
  matrix products  8.58 us (2%)
    psum x1, blocking collectives, shards(): density = lax.psum(partial_value, 'ky')  118 us
    all_gather x1, blocking collectives, shards(): every_row = lax.all_gather(charge, 'space', axis=0, tiled=True)  105 us
    all_to_all x1, waiting for transfers between devices, shards(): lax.all_to_all(mixed, 'ky', split_axis=1, concat_axis=2, tiled=True)  46.5 us
    ppermute x1, waiting for transfers between devices, with_halo(): lax.ppermute(lax.slice_in_dim(block, 0, width, axis=dim), axis, backward)  29.5 us
    all_to_all x1, starting transfers between devices, shards(): lax.all_to_all(distribution, 'ky', split_axis=2, concat_axis=1, tiled=True)  17 us
    ppermute x1, waiting for transfers between devices, with_halo(): lax.ppermute(lax.slice_in_dim(block, block.shape[dim] - width, None, axis...  8.73 us
  transfers between devices with their start and end apart: 4, of which 3 were waited for; matrix products, arithmetic and copies ran while one was open for 6% of the time, Pallas kernels for 0%

commit v1 on v0

--- a/solution.py
+++ b/solution.py
@@ -79,7 +79,13 @@
     sine_rows = sine_table(grid_rows)
     sine_cols = sine_table(col_count)
     eigen_cols = eigen_values(col_count)
-    every_row = lax.all_gather(charge, "space", axis=0, tiled=True)
+    history = []
+    for _ in range(lax.psum(1, "space")):
+        history.append(charge)
+    every_row = jnp.concatenate(
+        lax.all_to_all(jnp.stack(history, axis=0), axis_name="space", split_axis=0, concat_axis=0),
+        axis=0,
+    )
     along_x = jnp.dot(sine_rows, every_row, precision=precise)
     spectral = jnp.dot(along_x, sine_cols, precision=precise)
     spectral = spectral / (eigen_values(grid_rows)[:, None] + eigen_cols[None, :])

time: 379 us -> 321 us (0.85)
  the two profiles are of different devices: /device:TPU:32 before, /device:TPU:15 now
where the time goes in v1:
time: 321 us
  waiting for transfers between devices  176 us (55%)
  starting transfers between devices  67.1 us (21%)
  blocking collectives  34.2 us (11%)
  local copies, waits for them, and re-layouts  23.9 us (7%)
  other arithmetic  10.4 us (3%)
  matrix products  8.57 us (3%)
    ppermute x1, waiting for transfers between devices, with_halo(): lax.ppermute(lax.slice_in_dim(block, 0, width, axis=dim), axis, backward)  78.6 us
    all_to_all x1, waiting for transfers between devices, shards(): lax.all_to_all(distribution, 'ky', split_axis=2, concat_axis=1, tiled=True)  59.3 us
    psum x1, blocking collectives, shards(): density = lax.psum(partial_value, 'ky')  34.2 us
    all_to_all x1, waiting for transfers between devices, shards(): lax.all_to_all(mixed, 'ky', split_axis=1, concat_axis=2, tiled=True)  30.2 us
    ppermute x1, starting transfers between devices, with_halo(): lax.ppermute(lax.slice_in_dim(block, block.shape[dim] - width, None, axis...  20.6 us
    all_to_all x1, starting transfers between devices, shards(): lax.all_to_all(jnp.stack(history, axis=0), axis_name='space', split_axis=...  15.9 us
    all_to_all x1, starting transfers between devices, shards(): lax.all_to_all(distribution, 'ky', split_axis=2, concat_axis=1, tiled=True)  13.9 us
    ppermute x1, starting transfers between devices, with_halo(): lax.ppermute(lax.slice_in_dim(block, 0, width, axis=dim), axis, backward)  11.9 us
  transfers between devices with their start and end apart: 5, of which 4 were waited for; matrix products, arithmetic and copies ran while one was open for 7% of the time, Pallas kernels for 0%

profile of v1, /device:TPU:15, one launch (start us, length us, event | category | flops | bytes accessed | tf_op | source)
XLA Modules:
  0.0 320.9 jit_solution(15993424353270809283)
XLA Ops:
  0.0 1.9 reduce_sum.29
  1.9 34.2 %psum.7 = f32[1,256]{1,0:T(1,128)S(1)} all-reduce(f32[1,256]{1,0:T(1,128)S(1)} %bitcast.205), channel_id=1, replica_groups=mesh['space'=64,'ky'=8] {'ky'}, use_global_device_ids=true, to_apply=%region_1.0 | all-reduce | flops 256 | bytes 2048 | tf_op jit(solution)/shard_map/psum | solution.py:75
  36.3 0.7 stack.262
  37.0 15.9 %all-to-all-start.1 = ((f32[64,1,256]{2,1,0:T(1,128)}), f32[64,1,256]{2,1,0:T(1,128)S(1)}, u32[]{:S(2)}, u32[]{:S(2)}) async-start(f32[64,1,256]{2,1,0:T(1,128)} %stack.262), calls=%async_computation.1 | async-start | bytes 131072 | tf_op jit(solution)/shard_map/all_to_all | solution.py:86
  52.9 2.6 copy.28
  55.5 8.3 %all-to-all-done.1 = f32[64,1,256]{2,1,0:T(1,128)S(1)} async-done(((f32[64,1,256]{2,1,0:T(1,128)}), f32[64,1,256]{2,1,0:T(1,128)S(1)}, u32[]{:S(2)}, u32[]{:S(2)}) %all-to-all-start.1) | async-done | bytes 65568 | tf_op jit(solution)/shard_map/all_to_all | solution.py:86
  63.8 13.9 %all-to-all-start = ((f32[1,16,256,128]{3,1,0,2:T(8,128)}), f32[1,16,256,128]{3,1,0,2:T(8,128)}, u32[]{:S(2)}, u32[]{:S(2)}) async-start(f32[1,16,256,128]{3,1,0,2:T(8,128)} %copy.28), calls=%async_computation | async-start | bytes 4194304 | tf_op jit(solution)/shard_map/all_to_all | solution.py:95
  79.0 1.3 convolution_divide_fusion
  80.3 1.3 fusion.14
  89.9 1.9 mul.263
  91.8 2.7 mul.264
  94.5 59.3 %all-to-all-done = f32[1,16,256,128]{3,1,0,2:T(8,128)} async-done(((f32[1,16,256,128]{3,1,0,2:T(8,128)}), f32[1,16,256,128]{3,1,0,2:T(8,128)}, u32[]{:S(2)}, u32[]{:S(2)}) %all-to-all-start) | async-done | bytes 2097184 | tf_op jit(solution)/shard_map/all_to_all | solution.py:95
  153.8 2.4 copy.29
  156.2 2.1 fusion.1
  158.4 3.2 fusion.35
  161.6 3.1 copy.95
  164.7 4.7 %all-to-all-start.2 = ((f32[1,128,32,128]{3,2,0,1:T(8,128)}), f32[1,128,32,128]{3,2,0,1:T(8,128)}, u32[]{:S(2)}, u32[]{:S(2)}) async-start(f32[1,128,32,128]{3,2,0,1:T(8,128)} %copy.95), calls=%async_computation.2 | async-start | bytes 4194304 | tf_op jit(solution)/shard_map/all_to_all | solution.py:110
  169.5 11.9 %collective-permute-start.1 = (f32[1,16,256,128]{3,2,1,0:T(8,128)S(1)}, f32[1,16,256,128]{3,2,1,0:T(8,128)}, u32[]{:S(2)}, u32[]{:S(2)}) collective-permute-start(f32[1,16,256,128]{3,2,1,0:T(8,128)S(1)} %copy-done), channel_id=1, source_target_pairs={{8,0},{16,8},{24,16},{32,24},{40,32},{48,40},{56,48},{64,56},{72,6... | collective-permute-start | bytes 6291464 | tf_op jit(solution)/shard_map/ppermute | solution.py:21
  181.3 20.6 %collective-permute-start = (f32[1,16,256,128]{3,2,1,0:T(8,128)S(1)}, f32[1,16,256,128]{3,2,1,0:T(8,128)}, u32[]{:S(2)}, u32[]{:S(2)}) collective-permute-start(f32[1,16,256,128]{3,2,1,0:T(8,128)S(1)} %copy-done), channel_id=1, source_target_pairs={{0,8},{8,16},{16,24},{24,32},{32,40},{40,48},{48,56},{56,64},{64,7... | collective-permute-start | bytes 6291464 | tf_op jit(solution)/shard_map/ppermute | solution.py:18
  202.1 2.5 fusion.209
  204.6 30.2 %all-to-all-done.2 = f32[1,128,32,128]{3,2,0,1:T(8,128)} async-done(((f32[1,128,32,128]{3,2,0,1:T(8,128)}), f32[1,128,32,128]{3,2,0,1:T(8,128)}, u32[]{:S(2)}, u32[]{:S(2)}) %all-to-all-start.2) | async-done | bytes 2097184 | tf_op jit(solution)/shard_map/all_to_all | solution.py:110
  234.8 2.0 copy.96
  236.7 78.6 %collective-permute-done.1 = f32[1,16,256,128]{3,2,1,0:T(8,128)} collective-permute-done((f32[1,16,256,128]{3,2,1,0:T(8,128)S(1)}, f32[1,16,256,128]{3,2,1,0:T(8,128)}, u32[]{:S(2)}, u32[]{:S(2)}) %collective-permute-start.1) | collective-permute-done | bytes 2097184 | tf_op jit(solution)/shard_map/ppermute | solution.py:21
  315.4 5.5 %fusion.6 = f32[1,16,256,128]{3,2,1,0:T(8,128)} fusion(f32[1,16,256,128]{3,2,1,0:T(8,128)S(1)} %copy-done, f32[1,16,8,32,128]{4,3,2,1,0:T(8,128)S(1)} %copy.96, f32[1,16,255,128]{3,2,1,0:T(8,128)S(1)} %copy-done.3, f32[1,16,255,128]{3,2,1,0:T(8,128)S(1)} %copy-done.2, f32[1,16,256,128]{3,2,1,0:T(8,128)} %collective-permute-done, ...), kind=kLoop, calls=%fused_computation.8 | loop fusion | flops 7340032 | bytes 14674640 | tf_op jit(solution)/shard_map/add | solution.py:128
  (122 shorter events, 9.5 us)
Async XLA Ops:
  0.0 52.9 %copy-start = (f32[1,16,256,128]{3,2,1,0:T(8,128)S(1)}, f32[1,16,256,128]{3,2,1,0:T(8,128)}, u32[]{:S(2)}) copy-start(f32[1,16,256,128]{3,2,1,0:T(8,128)} %param.7) | copy-start | bytes 6291460
  0.0 36.2 %copy-start.6 = (f32[6]{0:T(128)S(1)}, f32[6]{0:T(128)}, u32[]{:S(2)}) copy-start(f32[6]{0:T(128)} %param.10) | copy-start | bytes 76
  0.0 36.2 %copy-start.7 = (f32[6]{0:T(128)S(1)}, f32[6]{0:T(128)}, u32[]{:S(2)}) copy-start(f32[6]{0:T(128)} %param.9) | copy-start | bytes 76
  0.0 36.2 %copy-start.5 = (s32[1,256]{1,0:T(1,128)S(1)}, s32[1,256]{1,0:T(1,128)}, u32[]{:S(2)}) copy-start(s32[1,256]{1,0:T(1,128)} %param.8) | copy-start | bytes 3076
  37.0 26.9 %all-to-all-start.1 = ((f32[64,1,256]{2,1,0:T(1,128)}), f32[64,1,256]{2,1,0:T(1,128)S(1)}, u32[]{:S(2)}, u32[]{:S(2)}) async-start(f32[64,1,256]{2,1,0:T(1,128)} %stack.262), calls=%async_computation.1 | async-start | bytes 131072 | tf_op jit(solution)/shard_map/all_to_all | solution.py:86
  63.8 90.0 %all-to-all-start = ((f32[1,16,256,128]{3,1,0,2:T(8,128)}), f32[1,16,256,128]{3,1,0,2:T(8,128)}, u32[]{:S(2)}, u32[]{:S(2)}) async-start(f32[1,16,256,128]{3,1,0,2:T(8,128)} %copy.28), calls=%async_computation | async-start | bytes 4194304 | tf_op jit(solution)/shard_map/all_to_all | solution.py:95
  153.8 2.4 copy-start.1
  164.7 37.3 %copy-start.8 = (f32[128]{0:T(128)S(1)}, f32[128]{0:T(128)}, u32[]{:S(2)}) copy-start(f32[128]{0:T(128)} %param.12) | copy-start | bytes 1540
  164.7 37.3 %copy-start.9 = (s32[128]{0:T(128)S(1)}, s32[128]{0:T(128)}, u32[]{:S(2)}) copy-start(s32[128]{0:T(128)} %param.13) | copy-start | bytes 1540
  164.7 70.0 %all-to-all-start.2 = ((f32[1,128,32,128]{3,2,0,1:T(8,128)}), f32[1,128,32,128]{3,2,0,1:T(8,128)}, u32[]{:S(2)}, u32[]{:S(2)}) async-start(f32[1,128,32,128]{3,2,0,1:T(8,128)} %copy.95), calls=%async_computation.2 | async-start | bytes 4194304 | tf_op jit(solution)/shard_map/all_to_all | solution.py:110
  169.5 145.9 %collective-permute-start.1 = (f32[1,16,256,128]{3,2,1,0:T(8,128)S(1)}, f32[1,16,256,128]{3,2,1,0:T(8,128)}, u32[]{:S(2)}, u32[]{:S(2)}) collective-permute-start(f32[1,16,256,128]{3,2,1,0:T(8,128)S(1)} %copy-done), channel_id=1, source_target_pairs={{8,0},{16,8},{24,16},{32,24},{40,32},{48,40},{56,48},{64,56},{72,6... | collective-permute-start | bytes 6291464 | tf_op jit(solution)/shard_map/ppermute | solution.py:21
  181.3 134.0 %collective-permute-start = (f32[1,16,256,128]{3,2,1,0:T(8,128)S(1)}, f32[1,16,256,128]{3,2,1,0:T(8,128)}, u32[]{:S(2)}, u32[]{:S(2)}) collective-permute-start(f32[1,16,256,128]{3,2,1,0:T(8,128)S(1)} %copy-done), channel_id=1, source_target_pairs={{0,8},{8,16},{16,24},{24,32},{32,40},{40,48},{48,56},{56,64},{64,7... | collective-permute-start | bytes 6291464 | tf_op jit(solution)/shard_map/ppermute | solution.py:18
  202.1 113.3 %copy-start.4 = (f32[16,128]{1,0:T(8,128)S(1)}, f32[16,128]{1,0:T(8,128)}, u32[]{:S(2)}) copy-start(f32[16,128]{1,0:T(8,128)} %param.11) | copy-start | bytes 24580
  234.8 80.6 %copy-start.2 = (f32[1,16,255,128]{3,2,1,0:T(8,128)S(1)}, f32[1,16,255,128]{3,2,1,0:T(8,128)}, u32[]{:S(2)}) copy-start(f32[1,16,255,128]{3,2,1,0:T(8,128)} %get-tuple-element.7) | copy-start | bytes 6266884
  234.8 80.6 %copy-start.3 = (f32[1,16,255,128]{3,2,1,0:T(8,128)S(1)}, f32[1,16,255,128]{3,2,1,0:T(8,128)}, u32[]{:S(2)}) copy-start(f32[1,16,255,128]{3,2,1,0:T(8,128)} %get-tuple-element.8) | copy-start | bytes 6266884
